TPU v7x, 512 devices: a whole 4x4x16 slice. The times are simulated.
512 devices in a mesh: row: 64 (over x, z), col: 8 (over y, core).
Axes of the slice: x: 4, y: 4, z: 16, core: 2. Of those that a mesh axis runs over, the one named last changes fastest.
Arguments:
- current: bfloat16 [2, 256, 32, 4, 128], P(None, 'row', 'col'), may hold values from -6 to 6
- probe: bfloat16 [2, 256, 32, 4, 128], P(None, 'row', 'col'), may hold values from -6 to 6
- near_list: int32 [256, 32, 2], P('row', 'col'), may hold values from 0 to 9, as said below
- near_blocks: bfloat16 [2, 256, 32, 2, 128, 128], P(None, 'row', 'col'), may hold values from -0.25 to 0.25
- radiation: bfloat16 [2, 128, 128], replicated, may hold values from -0.375 to 0.375
- reception: bfloat16 [2, 128, 128], replicated, may hold values from -0.375 to 0.375
- interp: float32 [256, 128], replicated, may hold values from -0.5 to 0.5
- phase: float32 [16, 256], replicated, may hold values from -3.140625 to 3.140625
- leaf_table: float32 [2, 15, 15, 128], replicated, may hold values from -0.36 to 0.36
- coarse_table: bfloat16 [2, 127, 15, 256], replicated, may hold values from -0.023925781 to 0.023925781
Outputs:
- forward_out: float32 [2, 256, 32, 4, 128], P(None, 'row', 'col')
- adjoint_out: float32 [2, 256, 32, 4, 128], P(None, 'row', 'col')
Inputs may be any that keep to these rules, and one draw needn't show every extreme that they name: `near_list`: the 2 slots of a box hold distinct codes; only slots after the first may be empty (code 9).
All inputs are finite; a program needn't handle non-finite values.
Results may differ from a plain program's by a relative error of at most 0.0027.
Values may be sent and summed in bfloat16 or wider, within the bound.
No kernel may reach another device: no remote copies, remote signals or barrier semaphores. Data moves between devices by JAX's collectives and lax.ppermute only.
A program may use at most 128 MiB of HBM per device.

v0:
```python
import jax
import jax.numpy as jnp
from jax import lax
from jax.sharding import PartitionSpec as P

HIGH = lax.Precision.HIGHEST


def with_halo(cells, sides, width):
    for axis, dim in sides:
        count = lax.axis_size(axis)
        ends = count - 1
        head = lax.slice_in_dim(cells, 0, width, axis=dim)
        tail = lax.slice_in_dim(cells, cells.shape[dim] - width, cells.shape[dim], axis=dim)
        cells = jnp.concatenate(
            [
                lax.ppermute(tail, axis, [(i, (i + 1) % count) for i in range(ends)]),
                cells,
                lax.ppermute(head, axis, [((i + 1) % count, i) for i in range(ends)]),
            ],
            axis=dim,
        )
    return cells


def from_behind(block, axis, distance):
    devices = range(lax.axis_size(axis))
    route = [(i - distance, i) for i in devices if i - distance in devices]
    return lax.ppermute(block, axis, route)


def complex_mul(left_re, left_im, right_re, right_im):
    return (left_re * right_re - left_im * right_im, left_re * right_im + left_im * right_re)


def conj_flip(table, axes):
    flipped = jnp.flip(table, axes)
    return jnp.stack([flipped[0], -flipped[1]])


def product(form, left, right):
    return jnp.einsum(form, left, right, preferred_element_type=jnp.float32)


def near_field(current, probe, near_list, near_blocks):
    box_side = current.shape[1]
    one_hot = (near_list[..., None] == jnp.arange(9)).astype(jnp.bfloat16)
    blocks_re = near_blocks[0]
    blocks_im = near_blocks[1]
    padded = with_halo(current, (("row", 1), ("col", 2)), 1)
    shifted = jnp.stack(
        [
            padded[
                :,
                offset_code // 3 : offset_code // 3 + box_side,
                offset_code % 3 : offset_code % 3 + box_side,
            ]
            for offset_code in range(9)
        ]
    )
    picked = product("rcko,oxrcmp->xkrcmp", one_hot, shifted).astype(jnp.bfloat16)
    fwd_re = product("rckpq,krcmq->rcmp", blocks_re, picked[0]) - product(
        "rckpq,krcmq->rcmp", blocks_im, picked[1]
    )
    fwd_im = product("rckpq,krcmq->rcmp", blocks_re, picked[1]) + product(
        "rckpq,krcmq->rcmp", blocks_im, picked[0]
    )
    near_fwd = jnp.stack([fwd_re, fwd_im])
    back_re = product("rckpq,rcmp->krcmq", blocks_re, probe[0]) + product(
        "rckpq,rcmp->krcmq", blocks_im, probe[1]
    )
    back_im = product("rckpq,rcmp->krcmq", blocks_re, probe[1]) - product(
        "rckpq,rcmp->krcmq", blocks_im, probe[0]
    )
    contrib = jnp.stack([back_re, back_im])
    placed_all = jnp.einsum(
        "rcko,xkrcmp->oxrcmp", one_hot.astype(jnp.float32), contrib, precision=HIGH
    )
    placed = jnp.zeros((2, box_side + 2, box_side + 2) + contrib.shape[4:], jnp.float32)
    for offset_code in range(9):
        placed = placed.at[
            :,
            offset_code // 3 : offset_code // 3 + box_side,
            offset_code % 3 : offset_code % 3 + box_side,
        ].add(placed_all[offset_code])
    for step_dir, send_row, keep_row in ((1, box_side + 1, 1), (-1, 0, box_side)):
        arrived = from_behind(placed[:, send_row], "row", step_dir)
        placed = placed.at[:, keep_row].add(arrived)
    for step_dir, send_col, keep_col in ((1, box_side + 1, 1), (-1, 0, box_side)):
        arrived = from_behind(placed[:, 1 : box_side + 1, send_col], "col", step_dir)
        placed = placed.at[:, 1 : box_side + 1, keep_col].add(arrived)
    return (near_fwd, placed[:, 1 : box_side + 1, 1 : box_side + 1])


def far_field(vectors, rad_tab, rcv_tab, leaf_tab, coarse_tab, interp, phase):
    box_side = vectors.shape[2]
    span = 3 * box_side
    reach = 2 * box_side - 1
    out_re = product("srcmp,sqp->srcmq", vectors[:, 0], rad_tab[:, 0]) - product(
        "srcmp,sqp->srcmq", vectors[:, 1], rad_tab[:, 1]
    )
    out_im = product("srcmp,sqp->srcmq", vectors[:, 0], rad_tab[:, 1]) + product(
        "srcmp,sqp->srcmq", vectors[:, 1], rad_tab[:, 0]
    )
    leaf_out = jnp.stack([out_re, out_im], 1)
    window = with_halo(leaf_out, (("row", 2), ("col", 3)), box_side)
    offsets = jnp.arange(2 * reach + 1) - reach
    near_offset = jnp.abs(offsets) <= 1
    keep = 1.0 - (near_offset[:, None] & near_offset[None, :]).astype(jnp.float32)
    masked = leaf_tab * keep[None, None, :, :, None]
    rows_in = []
    for row_pos in range(box_side):
        cols_in = []
        for col_pos in range(box_side):
            row_first = box_side - 1 - row_pos
            col_first = box_side - 1 - col_pos
            coeffs = masked[:, :, row_first : row_first + span, col_first : col_first + span]
            part_re, part_im = complex_mul(
                coeffs[:, 0, :, :, None], coeffs[:, 1, :, :, None], window[:, 0], window[:, 1]
            )
            cols_in.append(jnp.stack([part_re.sum((1, 2)), part_im.sum((1, 2))], 1))
        rows_in.append(jnp.stack(cols_in, 2))
    leaf_in = jnp.stack(rows_in, 2)
    interpolated = jnp.einsum("kq,sxrcmq->sxrcmk", interp, leaf_out, precision=HIGH)
    angles = phase.reshape(box_side, box_side, -1)
    cos_ph = jnp.cos(angles)[:, :, None, :]
    sin_ph = jnp.sin(angles)[:, :, None, :]
    top_re = (cos_ph * interpolated[:, 0] - sin_ph * interpolated[:, 1]).sum((1, 2))
    top_im = (cos_ph * interpolated[:, 1] + sin_ph * interpolated[:, 0]).sum((1, 2))
    top_b = jnp.stack([top_re, top_im], 1).astype(jnp.bfloat16)
    row_idx = lax.axis_index("row")
    col_idx = lax.axis_index("col")
    row_count = lax.axis_size("row")
    col_count = lax.axis_size("col")
    flat_tab = coarse_tab.reshape(
        coarse_tab.shape[0], 2, coarse_tab.shape[2] * coarse_tab.shape[3], coarse_tab.shape[4]
    )
    portion = lax.all_gather(top_b[:, :, None], ("row", "col"), axis=2, tiled=True)
    sources = jnp.arange(portion.shape[2])
    src_rows = sources // col_count
    src_cols = sources % col_count
    flat_index = (row_idx - src_rows + row_count - 1) * (2 * col_count - 1) + (
        col_idx - src_cols + col_count - 1
    )
    coeff = jnp.take(flat_tab, flat_index, axis=2).astype(jnp.float32)
    distant = ((jnp.abs(row_idx - src_rows) > 1) | (jnp.abs(col_idx - src_cols) > 1)).astype(
        jnp.float32
    )
    coef_re = coeff[:, 0] * distant[None, :, None]
    coef_im = coeff[:, 1] * distant[None, :, None]
    values = portion.astype(jnp.float32)
    got_re = jnp.einsum("snq,snmq->smq", coef_re, values[:, 0], precision=HIGH) - jnp.einsum(
        "snq,snmq->smq", coef_im, values[:, 1], precision=HIGH
    )
    got_im = jnp.einsum("snq,snmq->smq", coef_re, values[:, 1], precision=HIGH) + jnp.einsum(
        "snq,snmq->smq", coef_im, values[:, 0], precision=HIGH
    )
    coarse_in = jnp.stack([got_re, got_im], 1)
    in_re = coarse_in[:, 0][:, None, None]
    in_im = coarse_in[:, 1][:, None, None]
    back_re = cos_ph * in_re + sin_ph * in_im
    back_im = cos_ph * in_im - sin_ph * in_re
    spread = jnp.einsum(
        "kq,sxrcmk->sxrcmq", interp, jnp.stack([back_re, back_im], 1), precision=HIGH
    )
    incoming = (leaf_in + spread).astype(jnp.bfloat16)
    res_re = product("srcmq,spq->srcmp", incoming[:, 0], rcv_tab[:, 0]) - product(
        "srcmq,spq->srcmp", incoming[:, 1], rcv_tab[:, 1]
    )
    res_im = product("srcmq,spq->srcmp", incoming[:, 0], rcv_tab[:, 1]) + product(
        "srcmq,spq->srcmp", incoming[:, 1], rcv_tab[:, 0]
    )
    return jnp.stack([res_re, res_im], 1)


def per_device(
    current,
    probe,
    near_list,
    near_blocks,
    radiation,
    reception,
    interp,
    phase,
    leaf_table,
    coarse_table,
):
    near_fwd, near_adj = near_field(current, probe, near_list, near_blocks)
    fwd_set = (radiation, reception, leaf_table, coarse_table)
    adj_set = (
        jnp.stack([reception[0].T, -reception[1].T]),
        jnp.stack([radiation[0].T, -radiation[1].T]),
        conj_flip(leaf_table, (1, 2)),
        conj_flip(coarse_table, (1, 2)),
    )
    far_fwd = far_field(
        current[None],
        fwd_set[0][None],
        fwd_set[1][None],
        fwd_set[2][None],
        fwd_set[3][None],
        interp,
        phase,
    )[0]
    far_adj = far_field(
        probe[None],
        adj_set[0][None],
        adj_set[1][None],
        adj_set[2][None],
        adj_set[3][None],
        interp,
        phase,
    )[0]
    return (near_fwd + far_fwd, near_adj + far_adj)


def solution(mesh):
    placed = (
        P(None, "row", "col", None, None),
        P(None, "row", "col", None, None),
        P("row", "col", None),
        P(None, "row", "col", None, None, None),
        P(),
        P(),
        P(),
        P(),
        P(),
        P(),
    )
    return jax.shard_map(
        per_device,
        mesh=mesh,
        in_specs=placed,
        out_specs=(P(None, "row", "col", None, None), P(None, "row", "col", None, None)),
        check_vma=False,
    )
```

profile of v0, /device:TPU:1, one launch (start us, length us, event | category | flops | bytes accessed | tf_op | source)
XLA Modules:
  0.0 378.0 jit_solution(1067463419828961562)
XLA Ops:
  19.8 5.6 %collective-permute-start.4 = (f32[1,2,4,4,4,128]{5,4,3,2,1,0:T(4,128)}, f32[1,2,4,4,4,128]{5,4,3,2,1,0:T(4,128)}, u32[]{:S(2)}, u32[]{:S(2)}) collective-permute-start(f32[1,2,4,4,4,128]{5,4,3,2,1,0:T(4,128)} %pad_maximum_fusion.5), channel_id=1, source_target_pairs={{0,8},{8,16},{16,24},{24,32},{32,40},{40,48},{48,56},{56,64},{64,7... | collective-permute-start | bytes 196616 | tf_op jit(solution)/shard_map/ppermute | solution.py:17
  27.3 4.6 %collective-permute-start = (bf16[2,1,4,4,128]{4,3,2,1,0:T(4,128)(2,1)}, bf16[2,1,4,4,128]{4,3,2,1,0:T(4,128)(2,1)}, u32[]{:S(2)}, u32[]{:S(2)}) collective-permute-start(bf16[2,1,4,4,128]{4,3,2,1,0:T(4,128)(2,1)} %get-tuple-element.431), channel_id=1, source_target_pairs={{0,8},{8,16},{16,24},{24,32},{32,40},{40,48},{48,56},{56,64},{64,7... | collective-permute-start | bytes 24584 | tf_op jit(solution)/shard_map/ppermute | solution.py:17
  35.5 1.9 fusion.131
  42.6 1.6 fusion.128
  45.5 6.5 %fusion.125 = (bf16[1,127,15,256]{3,0,2,1:T(2,128)(2,1)}, bf16[1,127,15,256]{3,0,2,1:T(2,128)(2,1)S(1)}) fusion(bf16[2,127,15,256]{3,0,2,1:T(2,128)(2,1)} %param.47), kind=kLoop, calls=%fused_computation.445 | loop fusion | bytes 3901440 | tf_op jit(solution)/shard_map/slice | solution.py:38
  52.0 3.3 reverse_negate_fusion
  55.3 4.8 %slice.1246 = bf16[1,127,15,256]{3,0,2,1:T(2,128)(2,1)} reverse(bf16[1,127,15,256]{3,0,2,1:T(2,128)(2,1)} %get-tuple-element.295), dimensions={1,2} | reverse | bytes 1950720 | tf_op jit(solution)/shard_map/slice | solution.py:38
  60.1 6.5 %maximum_bitcast_fusion = bf16[2,1905,256]{2,0,1:T(2,128)(2,1)} fusion(bf16[1,1,1905,256]{3,1,2,0:T(2,128)(2,1)} %bitcast.1058, bf16[1,1,1905,256]{3,1,2,0:T(2,128)(2,1)} %bitcast.1059), kind=kLoop, calls=%fused_computation.18 | loop fusion | flops 3901440 | bytes 3901440 | tf_op jit(solution)/shard_map/jit(_take)/Arg_0.13 | solution.py:145
  66.7 4.3 %gather_fusion.1 = bf16[512,2,256]{2,1,0:T(2,128)(2,1)} fusion(bf16[2,1905,256]{2,0,1:T(2,128)(2,1)} %maximum_bitcast_fusion, s32[1024]{0:T(1024)S(1)} %pad_clamp_fusion), kind=kCustom, calls=%fused_computation.1.clone | custom fusion | bytes 1050624 | tf_op jit(solution)/shard_map/jit(_take)/gather | solution.py:145
  70.9 4.3 %gather_fusion = bf16[512,2,256]{2,1,0:T(2,128)(2,1)} fusion(bf16[2,1905,256]{2,0,1:T(2,128)(2,1)} %bitcast.1057, s32[1024]{0:T(1024)S(1)} %pad_clamp_fusion), kind=kCustom, calls=%fused_computation.clone | custom fusion | bytes 1050624 | tf_op jit(solution)/shard_map/jit(_take)/gather | solution.py:145
  76.5 3.3 fusion.45
  79.8 1.8 fusion.127
  88.3 1.6 copy_bitcast_fusion.45
  90.0 1.6 copy_bitcast_fusion.43
  91.6 1.6 copy_bitcast_fusion.41
  93.2 1.7 copy_bitcast_fusion.33
  94.9 1.6 copy_bitcast_fusion.51
  96.6 1.7 copy_bitcast_fusion.49
  107.5 1.9 fusion.63
  109.7 1.6 fusion.49
  115.1 8.9 %collective-permute-start.3 = (bf16[2,6,1,4,128]{4,3,2,1,0:T(4,128)(2,1)S(1)}, bf16[2,6,1,4,128]{4,3,2,1,0:T(4,128)(2,1)S(1)}, u32[]{:S(2)}, u32[]{:S(2)}) collective-permute-start(bf16[2,6,1,4,128]{4,3,2,1,0:T(4,128)(2,1)S(1)} %get-tuple-element.419), channel_id=1, source_target_pairs={{1,0},{2,1},{3,2},{4,3},{5,4},{6,5},{7,6},{9,8},{10,9},{11,10},{12... | collective-permute-start | bytes 36872 | tf_op jit(solution)/shard_map/ppermute | solution.py:19
  124.0 1.9 collective-permute-start.2
  128.2 1.6 copy.524
  129.7 1.6 copy.525
  131.3 1.6 copy.522
  132.9 1.6 copy.523
  134.4 1.6 copy.520
  136.0 1.6 copy.521
  137.5 1.6 copy.512
  139.1 1.6 copy.513
  140.7 1.5 copy.530
  142.2 1.5 copy.531
  150.2 1.5 copy.542
  151.7 1.5 copy.543
  159.8 4.9 %collective-permute-start.12 = (f32[1,2,4,4,4,128]{5,4,3,2,1,0:T(4,128)}, f32[1,2,4,4,4,128]{5,4,3,2,1,0:T(4,128)}, u32[]{:S(2)}, u32[]{:S(2)}) collective-permute-start(f32[1,2,4,4,4,128]{5,4,3,2,1,0:T(4,128)} %pad_maximum_fusion.6), channel_id=1, source_target_pairs={{0,8},{8,16},{16,24},{24,32},{32,40},{40,48},{48,56},{56,64},{64,7... | collective-permute-start | bytes 196616 | tf_op jit(solution)/shard_map/ppermute | solution.py:17
  164.7 1.9 collective-permute-start.8
  168.3 2.5 stack.593
  176.8 2.2 collective-permute-done.9
  179.0 2.3 collective-permute-start.10
  182.2 2.8 collective-permute-start.7
  185.1 2.7 collective-permute-start.6
  187.8 1.9 collective-permute-start.11
  190.7 1.9 collective-permute-start.15
  192.6 3.9 %collective-permute-start.14 = (f32[1,2,12,4,4,128]{5,4,3,2,1,0:T(4,128)S(1)}, f32[1,2,12,4,4,128]{5,4,3,2,1,0:T(4,128)S(1)}, u32[]{:S(2)}, u32[]{:S(2)}) collective-permute-start(f32[1,2,12,4,4,128]{5,4,3,2,1,0:T(4,128)S(1)} %pad_maximum_fusion.3), channel_id=1, source_target_pairs={{0,1},{1,2},{2,3},{3,4},{4,5},{5,6},{6,7},{8,9},{9,10},{10,11},{11... | collective-permute-start | bytes 589832 | tf_op jit(solution)/shard_map/ppermute | solution.py:17
  203.1 1.8 subtract_reduce_fusion.6
  207.9 3.2 fusion.6
  211.2 153.4 %all-gather.3.cloned.1.call-done = bf16[1,2,512,4,256]{4,3,2,1,0:T(4,128)(2,1)} async-done(((bf16[1,2,1,4,256]{4,3,2,1,0:T(4,128)(2,1)}), bf16[1,2,512,4,256]{4,3,2,1,0:T(4,128)(2,1)}) %all-gather.3.cloned.1.call-update) | async-done | bytes 2097168 | tf_op jit(solution)/shard_map/all_gather | solution.py:138
  364.6 3.2 fusion.2
  (489 shorter events, 81.8 us)
Async XLA Ops:
  7.2 27.9 %copy-start.8 = (f32[2,15,15,128]{3,0,2,1:T(2,128)S(1)}, f32[2,15,15,128]{3,0,2,1:T(2,128)}, u32[]{:S(2)}) copy-start(f32[2,15,15,128]{3,0,2,1:T(2,128)} %param.46) | copy-start | bytes 691204
  7.2 200.7 %all-gather.5.cloned.1.call-start = ((), (), s32[]{:S(2)}) async-start(), calls=%async_computation.1 | async-start | bytes 2101248 | tf_op jit(solution)/shard_map/all_gather | solution.py:138
  17.8 346.8 %all-gather.3.cloned.1.call-start = ((), (), s32[]{:S(2)}) async-start(), calls=%async_computation | async-start | bytes 2101248 | tf_op jit(solution)/shard_map/all_gather | solution.py:138
  18.5 162.8 %collective-permute-start.5 = (f32[1,2,4,4,4,128]{5,4,3,2,1,0:T(4,128)}, f32[1,2,4,4,4,128]{5,4,3,2,1,0:T(4,128)}, u32[]{:S(2)}, u32[]{:S(2)}) collective-permute-start(f32[1,2,4,4,4,128]{5,4,3,2,1,0:T(4,128)} %pad_maximum_fusion.5), channel_id=1, source_target_pairs={{8,0},{16,8},{24,16},{32,24},{40,32},{48,40},{56,48},{64,56},{72,6... | collective-permute-start | bytes 196616 | tf_op jit(solution)/shard_map/ppermute | solution.py:19
  19.8 161.5 %collective-permute-start.4 = (f32[1,2,4,4,4,128]{5,4,3,2,1,0:T(4,128)}, f32[1,2,4,4,4,128]{5,4,3,2,1,0:T(4,128)}, u32[]{:S(2)}, u32[]{:S(2)}) collective-permute-start(f32[1,2,4,4,4,128]{5,4,3,2,1,0:T(4,128)} %pad_maximum_fusion.5), channel_id=1, source_target_pairs={{0,8},{8,16},{16,24},{24,32},{32,40},{40,48},{48,56},{56,64},{64,7... | collective-permute-start | bytes 196616 | tf_op jit(solution)/shard_map/ppermute | solution.py:17
  26.0 87.4 %collective-permute-start.1 = (bf16[2,1,4,4,128]{4,3,2,1,0:T(4,128)(2,1)}, bf16[2,1,4,4,128]{4,3,2,1,0:T(4,128)(2,1)}, u32[]{:S(2)}, u32[]{:S(2)}) collective-permute-start(bf16[2,1,4,4,128]{4,3,2,1,0:T(4,128)(2,1)} %get-tuple-element.430), channel_id=1, source_target_pairs={{8,0},{16,8},{24,16},{32,24},{40,32},{48,40},{56,48},{64,56},{72,6... | collective-permute-start | bytes 24584 | tf_op jit(solution)/shard_map/ppermute | solution.py:19
  27.3 85.4 %collective-permute-start = (bf16[2,1,4,4,128]{4,3,2,1,0:T(4,128)(2,1)}, bf16[2,1,4,4,128]{4,3,2,1,0:T(4,128)(2,1)}, u32[]{:S(2)}, u32[]{:S(2)}) collective-permute-start(bf16[2,1,4,4,128]{4,3,2,1,0:T(4,128)(2,1)} %get-tuple-element.431), channel_id=1, source_target_pairs={{0,8},{8,16},{16,24},{24,32},{32,40},{40,48},{48,56},{56,64},{64,7... | collective-permute-start | bytes 24584 | tf_op jit(solution)/shard_map/ppermute | solution.py:17
  32.5 157.2 %collective-permute-start.13 = (f32[1,2,4,4,4,128]{5,4,3,2,1,0:T(4,128)}, f32[1,2,4,4,4,128]{5,4,3,2,1,0:T(4,128)}, u32[]{:S(2)}, u32[]{:S(2)}) collective-permute-start(f32[1,2,4,4,4,128]{5,4,3,2,1,0:T(4,128)} %pad_maximum_fusion.6), channel_id=1, source_target_pairs={{8,0},{16,8},{24,16},{32,24},{40,32},{48,40},{56,48},{64,56},{72,6... | collective-permute-start | bytes 196616 | tf_op jit(solution)/shard_map/ppermute | solution.py:19
  45.5 36.6 %copy-start.132 = (s32[4,4,2]{2,1,0:T(4,128)}, s32[4,4,2]{2,1,0:T(4,128)S(1)}, u32[]{:S(2)}) copy-start(s32[4,4,2]{2,1,0:T(4,128)S(1)} %copy.258) | copy-start | bytes 388
  111.2 32.5 %copy-start.84 = (f32[1,1,12,12,128]{4,0,3,2,1:T(1,128)S(1)}, f32[1,1,12,12,128]{4,0,3,2,1:T(1,128)}, u32[]{:S(2)}) copy-start(f32[1,1,12,12,128]{4,0,3,2,1:T(1,128)} %get-tuple-element.355) | copy-start | bytes 221188
  111.2 33.1 %copy-start.83 = (f32[1,1,12,12,128]{4,0,3,2,1:T(1,128)S(1)}, f32[1,1,12,12,128]{4,0,3,2,1:T(1,128)}, u32[]{:S(2)}) copy-start(f32[1,1,12,12,128]{4,0,3,2,1:T(1,128)} %get-tuple-element.356) | copy-start | bytes 221188
  111.2 33.8 %copy-start.82 = (f32[1,1,12,12,128]{4,0,3,2,1:T(1,128)S(1)}, f32[1,1,12,12,128]{4,0,3,2,1:T(1,128)}, u32[]{:S(2)}) copy-start(f32[1,1,12,12,128]{4,0,3,2,1:T(1,128)} %get-tuple-element.353) | copy-start | bytes 221188
  111.2 34.4 %copy-start.81 = (f32[1,1,12,12,128]{4,0,3,2,1:T(1,128)S(1)}, f32[1,1,12,12,128]{4,0,3,2,1:T(1,128)}, u32[]{:S(2)}) copy-start(f32[1,1,12,12,128]{4,0,3,2,1:T(1,128)} %get-tuple-element.354) | copy-start | bytes 221188
  111.2 35.1 %copy-start.80 = (f32[1,1,12,12,128]{4,0,3,2,1:T(1,128)S(1)}, f32[1,1,12,12,128]{4,0,3,2,1:T(1,128)}, u32[]{:S(2)}) copy-start(f32[1,1,12,12,128]{4,0,3,2,1:T(1,128)} %get-tuple-element.341) | copy-start | bytes 221188
  111.2 35.7 %copy-start.79 = (f32[1,1,12,12,128]{4,0,3,2,1:T(1,128)S(1)}, f32[1,1,12,12,128]{4,0,3,2,1:T(1,128)}, u32[]{:S(2)}) copy-start(f32[1,1,12,12,128]{4,0,3,2,1:T(1,128)} %get-tuple-element.342) | copy-start | bytes 221188
  111.2 36.3 %copy-start.78 = (f32[1,1,12,12,128]{4,0,3,2,1:T(1,128)S(1)}, f32[1,1,12,12,128]{4,0,3,2,1:T(1,128)}, u32[]{:S(2)}) copy-start(f32[1,1,12,12,128]{4,0,3,2,1:T(1,128)} %get-tuple-element.343) | copy-start | bytes 221188
  111.3 37.0 %copy-start.77 = (f32[1,1,12,12,128]{4,0,3,2,1:T(1,128)S(1)}, f32[1,1,12,12,128]{4,0,3,2,1:T(1,128)}, u32[]{:S(2)}) copy-start(f32[1,1,12,12,128]{4,0,3,2,1:T(1,128)} %get-tuple-element.344) | copy-start | bytes 221188
  111.3 37.6 %copy-start.76 = (f32[1,1,12,12,128]{4,0,3,2,1:T(1,128)S(1)}, f32[1,1,12,12,128]{4,0,3,2,1:T(1,128)}, u32[]{:S(2)}) copy-start(f32[1,1,12,12,128]{4,0,3,2,1:T(1,128)} %get-tuple-element.345) | copy-start | bytes 221188
  111.3 38.3 %copy-start.75 = (f32[1,1,12,12,128]{4,0,3,2,1:T(1,128)S(1)}, f32[1,1,12,12,128]{4,0,3,2,1:T(1,128)}, u32[]{:S(2)}) copy-start(f32[1,1,12,12,128]{4,0,3,2,1:T(1,128)} %get-tuple-element.346) | copy-start | bytes 221188
  114.4 38.8 %copy-start.102 = (f32[1,1,12,12,128]{4,0,3,2,1:T(1,128)S(1)}, f32[1,1,12,12,128]{4,0,3,2,1:T(1,128)}, u32[]{:S(2)}) copy-start(f32[1,1,12,12,128]{4,0,3,2,1:T(1,128)} %get-tuple-element.366) | copy-start | bytes 221188
  115.1 44.6 %collective-permute-start.3 = (bf16[2,6,1,4,128]{4,3,2,1,0:T(4,128)(2,1)S(1)}, bf16[2,6,1,4,128]{4,3,2,1,0:T(4,128)(2,1)S(1)}, u32[]{:S(2)}, u32[]{:S(2)}) collective-permute-start(bf16[2,6,1,4,128]{4,3,2,1,0:T(4,128)(2,1)S(1)} %get-tuple-element.419), channel_id=1, source_target_pairs={{1,0},{2,1},{3,2},{4,3},{5,4},{6,5},{7,6},{9,8},{10,9},{11,10},{12... | collective-permute-start | bytes 36872 | tf_op jit(solution)/shard_map/ppermute | solution.py:19
  124.0 40.7 %collective-permute-start.2 = (bf16[2,6,1,4,128]{4,3,2,1,0:T(4,128)(2,1)S(1)}, bf16[2,6,1,4,128]{4,3,2,1,0:T(4,128)(2,1)S(1)}, u32[]{:S(2)}, u32[]{:S(2)}) collective-permute-start(bf16[2,6,1,4,128]{4,3,2,1,0:T(4,128)(2,1)S(1)} %get-tuple-element.420), channel_id=1, source_target_pairs={{0,1},{1,2},{2,3},{3,4},{4,5},{5,6},{6,7},{8,9},{9,10},{10,11},{11... | collective-permute-start | bytes 36872 | tf_op jit(solution)/shard_map/ppermute | solution.py:17
  125.9 27.9 %copy-start.101 = (f32[1,1,12,12,128]{4,0,3,2,1:T(1,128)S(1)}, f32[1,1,12,12,128]{4,0,3,2,1:T(1,128)}, u32[]{:S(2)}) copy-start(f32[1,1,12,12,128]{4,0,3,2,1:T(1,128)} %get-tuple-element.367) | copy-start | bytes 221188
  128.2 26.3 %copy-start.100 = (f32[1,1,12,12,128]{4,0,3,2,1:T(1,128)S(1)}, f32[1,1,12,12,128]{4,0,3,2,1:T(1,128)}, u32[]{:S(2)}) copy-start(f32[1,1,12,12,128]{4,0,3,2,1:T(1,128)} %get-tuple-element.357) | copy-start | bytes 221188
  129.7 25.4 %copy-start.74 = (f32[1,1,12,12,128]{4,0,3,2,1:T(1,128)S(1)}, f32[1,1,12,12,128]{4,0,3,2,1:T(1,128)}, u32[]{:S(2)}) copy-start(f32[1,1,12,12,128]{4,0,3,2,1:T(1,128)} %get-tuple-element.338) | copy-start | bytes 221188
  131.3 24.5 %copy-start.99 = (f32[1,1,12,12,128]{4,0,3,2,1:T(1,128)S(1)}, f32[1,1,12,12,128]{4,0,3,2,1:T(1,128)}, u32[]{:S(2)}) copy-start(f32[1,1,12,12,128]{4,0,3,2,1:T(1,128)} %get-tuple-element.360) | copy-start | bytes 221188
  159.8 30.0 %collective-permute-start.12 = (f32[1,2,4,4,4,128]{5,4,3,2,1,0:T(4,128)}, f32[1,2,4,4,4,128]{5,4,3,2,1,0:T(4,128)}, u32[]{:S(2)}, u32[]{:S(2)}) collective-permute-start(f32[1,2,4,4,4,128]{5,4,3,2,1,0:T(4,128)} %pad_maximum_fusion.6), channel_id=1, source_target_pairs={{0,8},{8,16},{16,24},{24,32},{32,40},{40,48},{48,56},{56,64},{64,7... | collective-permute-start | bytes 196616 | tf_op jit(solution)/shard_map/ppermute | solution.py:17
  164.7 8.9 %collective-permute-start.8 = (f32[2,6,4,128]{3,2,0,1:T(4,128)}, f32[2,6,4,128]{3,2,0,1:T(4,128)}, u32[]{:S(2)}, u32[]{:S(2)}) collective-permute-start(f32[2,6,4,128]{3,2,0,1:T(4,128)} %slice_bitcast_fusion.41), channel_id=1, source_target_pairs={{0,8},{8,16},{16,24},{24,32},{32,40},{40,48},{48,56},{56,64},{64,7... | collective-permute-start | bytes 73736 | tf_op jit(solution)/shard_map/ppermute | solution.py:29
  173.2 24.8 %copy-start.62 = (f32[12,12,128]{2,1,0:T(8,128)S(1)}, f32[12,12,128]{2,1,0:T(8,128)}, u32[]{:S(2)}) copy-start(f32[12,12,128]{2,1,0:T(8,128)} %get-tuple-element.454) | copy-start | bytes 221188
  173.2 24.8 %copy-start.63 = (f32[12,12,128]{2,1,0:T(8,128)S(1)}, f32[12,12,128]{2,1,0:T(8,128)}, u32[]{:S(2)}) copy-start(f32[12,12,128]{2,1,0:T(8,128)} %get-tuple-element.455) | copy-start | bytes 221188
  173.2 24.8 %copy-start.64 = (f32[12,12,128]{2,1,0:T(8,128)S(1)}, f32[12,12,128]{2,1,0:T(8,128)}, u32[]{:S(2)}) copy-start(f32[12,12,128]{2,1,0:T(8,128)} %get-tuple-element.452) | copy-start | bytes 221188
  173.2 24.8 %copy-start.65 = (f32[12,12,128]{2,1,0:T(8,128)S(1)}, f32[12,12,128]{2,1,0:T(8,128)}, u32[]{:S(2)}) copy-start(f32[12,12,128]{2,1,0:T(8,128)} %get-tuple-element.453) | copy-start | bytes 221188
  173.2 24.8 %copy-start.66 = (f32[12,12,128]{2,1,0:T(8,128)S(1)}, f32[12,12,128]{2,1,0:T(8,128)}, u32[]{:S(2)}) copy-start(f32[12,12,128]{2,1,0:T(8,128)} %get-tuple-element.450) | copy-start | bytes 221188
  173.2 24.8 %copy-start.67 = (f32[12,12,128]{2,1,0:T(8,128)S(1)}, f32[12,12,128]{2,1,0:T(8,128)}, u32[]{:S(2)}) copy-start(f32[12,12,128]{2,1,0:T(8,128)} %get-tuple-element.451) | copy-start | bytes 221188
  173.2 24.8 %copy-start.68 = (f32[12,12,128]{2,1,0:T(8,128)S(1)}, f32[12,12,128]{2,1,0:T(8,128)}, u32[]{:S(2)}) copy-start(f32[12,12,128]{2,1,0:T(8,128)} %get-tuple-element.442) | copy-start | bytes 221188
  173.2 24.8 %copy-start.69 = (f32[12,12,128]{2,1,0:T(8,128)S(1)}, f32[12,12,128]{2,1,0:T(8,128)}, u32[]{:S(2)}) copy-start(f32[12,12,128]{2,1,0:T(8,128)} %get-tuple-element.443) | copy-start | bytes 221188
  174.4 4.6 %collective-permute-start.9 = (f32[2,6,4,128]{3,2,0,1:T(4,128)S(1)}, f32[2,6,4,128]{3,2,0,1:T(4,128)S(1)}, u32[]{:S(2)}, u32[]{:S(2)}) collective-permute-start(f32[2,6,4,128]{3,2,0,1:T(4,128)S(1)} %slice_bitcast_fusion.40), channel_id=1, source_target_pairs={{8,0},{16,8},{24,16},{32,24},{40,32},{48,40},{56,48},{64,56},{72,6... | collective-permute-start | bytes 73736 | tf_op jit(solution)/shard_map/ppermute | solution.py:29
  179.0 8.8 %collective-permute-start.10 = (f32[2,4,4,128]{3,2,0,1:T(4,128)S(1)}, f32[2,4,4,128]{3,2,0,1:T(4,128)S(1)}, u32[]{:S(2)}, u32[]{:S(2)}) collective-permute-start(f32[2,4,4,128]{3,2,0,1:T(4,128)S(1)} %slice_bitcast_fusion.47), channel_id=1, source_target_pairs={{0,1},{1,2},{2,3},{3,4},{4,5},{5,6},{6,7},{8,9},{9,10},{10,11},{11... | collective-permute-start | bytes 49160 | tf_op jit(solution)/shard_map/ppermute | solution.py:29
  182.2 14.5 %collective-permute-start.7 = (f32[1,2,12,4,4,128]{5,4,3,2,1,0:T(4,128)S(1)}, f32[1,2,12,4,4,128]{5,4,3,2,1,0:T(4,128)S(1)}, u32[]{:S(2)}, u32[]{:S(2)}) collective-permute-start(f32[1,2,12,4,4,128]{5,4,3,2,1,0:T(4,128)S(1)} %pad_maximum_fusion.2), channel_id=1, source_target_pairs={{1,0},{2,1},{3,2},{4,3},{5,4},{6,5},{7,6},{9,8},{10,9},{11,10},{12... | collective-permute-start | bytes 589832 | tf_op jit(solution)/shard_map/ppermute | solution.py:19
  185.1 11.6 %collective-permute-start.6 = (f32[1,2,12,4,4,128]{5,4,3,2,1,0:T(4,128)S(1)}, f32[1,2,12,4,4,128]{5,4,3,2,1,0:T(4,128)S(1)}, u32[]{:S(2)}, u32[]{:S(2)}) collective-permute-start(f32[1,2,12,4,4,128]{5,4,3,2,1,0:T(4,128)S(1)} %pad_maximum_fusion.2), channel_id=1, source_target_pairs={{0,1},{1,2},{2,3},{3,4},{4,5},{5,6},{6,7},{8,9},{9,10},{10,11},{11... | collective-permute-start | bytes 589832 | tf_op jit(solution)/shard_map/ppermute | solution.py:17
  187.8 8.7 %collective-permute-start.11 = (f32[2,4,4,128]{3,2,0,1:T(4,128)S(1)}, f32[2,4,4,128]{3,2,0,1:T(4,128)S(1)}, u32[]{:S(2)}, u32[]{:S(2)}) collective-permute-start(f32[2,4,4,128]{3,2,0,1:T(4,128)S(1)} %slice_bitcast_fusion.46), channel_id=1, source_target_pairs={{1,0},{2,1},{3,2},{4,3},{5,4},{6,5},{7,6},{9,8},{10,9},{11,10},{12... | collective-permute-start | bytes 49160 | tf_op jit(solution)/shard_map/ppermute | solution.py:29
  190.7 11.1 %collective-permute-start.15 = (f32[1,2,12,4,4,128]{5,4,3,2,1,0:T(4,128)S(1)}, f32[1,2,12,4,4,128]{5,4,3,2,1,0:T(4,128)S(1)}, u32[]{:S(2)}, u32[]{:S(2)}) collective-permute-start(f32[1,2,12,4,4,128]{5,4,3,2,1,0:T(4,128)S(1)} %pad_maximum_fusion.3), channel_id=1, source_target_pairs={{1,0},{2,1},{3,2},{4,3},{5,4},{6,5},{7,6},{9,8},{10,9},{11,10},{12... | collective-permute-start | bytes 589832 | tf_op jit(solution)/shard_map/ppermute | solution.py:19
  192.6 9.2 %collective-permute-start.14 = (f32[1,2,12,4,4,128]{5,4,3,2,1,0:T(4,128)S(1)}, f32[1,2,12,4,4,128]{5,4,3,2,1,0:T(4,128)S(1)}, u32[]{:S(2)}, u32[]{:S(2)}) collective-permute-start(f32[1,2,12,4,4,128]{5,4,3,2,1,0:T(4,128)S(1)} %pad_maximum_fusion.3), channel_id=1, source_target_pairs={{0,1},{1,2},{2,3},{3,4},{4,5},{5,6},{6,7},{8,9},{9,10},{10,11},{11... | collective-permute-start | bytes 589832 | tf_op jit(solution)/shard_map/ppermute | solution.py:17
  207.6 157.0 %copy-start.2 = (f32[256,512]{0,1:T(8,128)S(1)}, f32[256,512]{0,1:T(8,128)}, u32[]{:S(2)}) copy-start(f32[256,512]{0,1:T(8,128)} %get-tuple-element.434) | copy-start | bytes 1572868
  207.7 157.0 %copy-start.3 = (f32[256,512]{0,1:T(8,128)S(1)}, f32[256,512]{0,1:T(8,128)}, u32[]{:S(2)}) copy-start(f32[256,512]{0,1:T(8,128)} %get-tuple-element.435) | copy-start | bytes 1572868
  211.1 156.7 %copy-start.127 = (f32[4,4,256]{2,1,0:T(4,128)S(1)}, f32[4,4,256]{2,1,0:T(4,128)}, u32[]{:S(2)}) copy-start(f32[4,4,256]{2,1,0:T(4,128)} %copy-done.126) | copy-start | bytes 49156
  211.1 156.7 %copy-start.129 = (f32[4,4,256]{2,1,0:T(4,128)S(1)}, f32[4,4,256]{2,1,0:T(4,128)}, u32[]{:S(2)}) copy-start(f32[4,4,256]{2,1,0:T(4,128)} %copy-done.128) | copy-start | bytes 49156
  211.2 157.1 %copy-start.11 = (bf16[2,128,128]{2,1,0:T(8,128)(2,1)S(1)}, bf16[2,128,128]{2,1,0:T(8,128)(2,1)}, u32[]{:S(2)}) copy-start(bf16[2,128,128]{2,1,0:T(8,128)(2,1)} %param.43) | copy-start | bytes 196612
  (109 other events, 1101.1 us)
Sparse Core Ops, SparseCore 0:
  17.9 175.8 all-gather.4
  198.5 166.0 all-gather.2
where the time goes:
time: 381 us; the launch traced here: 378 us
  waiting for transfers between devices  156 us (41%)
  local copies, waits for them, and re-layouts  93.3 us (24%)
  starting transfers between devices  48.6 us (13%)
  other arithmetic  47.6 us (12%)
  matrix products  16.4 us (4%)
  between operations  16.4 us (4%)
    all_gather x2, waiting for transfers between devices, far_field(): lax.all_gather(top_b[:, :, None], ('row', 'col'), axis=2, tiled=True)  153 us
    unnamed x333, local copies, waits for them, and re-layouts  52.9 us
    ppermute x6, starting transfers between devices, with_halo(): lax.ppermute(tail, axis, [(i, (i + 1) % count) for i in range(ends)])  23.6 us
    ppermute x6, starting transfers between devices, with_halo(): lax.ppermute(head, axis, [((i + 1) % count, i) for i in range(ends)])  17.5 us
    dot_general x25, matrix products, product(): return jnp.einsum(form, left, right, preferred_element_type=jnp.float32)  14.3 us
    slice x3, local copies, waits for them, and re-layouts, conj_flip(): return jnp.stack([flipped[0], -flipped[1]])  11.5 us
    gather x2, local copies, waits for them, and re-layouts, far_field(): coeff = jnp.take(flat_tab, flat_index, axis=2).astype(jnp.float32)  8.56 us
  transfers between devices with their start and end apart: 18, of which 2 were waited for; matrix products, arithmetic and copies ran while one was open for 37% of the time, Pallas kernels for 0%

commit v1 on v0

--- a/solution.py
+++ b/solution.py
@@ -135,7 +135,12 @@
     flat_tab = coarse_tab.reshape(
         coarse_tab.shape[0], 2, coarse_tab.shape[2] * coarse_tab.shape[3], coarse_tab.shape[4]
     )
-    portion = lax.all_gather(top_b[:, :, None], ("row", "col"), axis=2, tiled=True)
+    portion = jnp.concatenate(
+        lax.all_to_all(
+            jnp.stack([top_b[:, :, None]] * lax.axis_size(("row", "col"))), ("row", "col"), 0, 0
+        ),
+        axis=2,
+    )
     sources = jnp.arange(portion.shape[2])
     src_rows = sources // col_count
     src_cols = sources % col_count

time: 381 us -> 313 us (0.82)
  waiting for transfers between devices: 156 us -> 71.8 us
  starting transfers between devices: 48.6 us -> 96.5 us
  local copies, waits for them, and re-layouts: 93.3 us -> 78.8 us
  between operations: 16.4 us -> 3.08 us
  other arithmetic: 47.6 us -> 41.9 us
    all_gather x2 -> x0, waiting for transfers between devices: 153 us -> none  [far_field(): lax.all_gather(top_b[:, :, None], ('row', 'col'), axis=2, tiled=True)]
    all_to_all x0 -> x2, waiting for transfers between devices: none -> 69.5 us  [far_field(): lax.all_to_all(jnp.stack([top_b[:, :, None]] * lax.axis_size(('row', 'col...]
    all_to_all x0 -> x2, starting transfers between devices: none -> 47.5 us  [far_field(): lax.all_to_all(jnp.stack([top_b[:, :, None]] * lax.axis_size(('row', 'col...]
    unnamed x333 -> x239, local copies, waits for them, and re-layouts: 52.9 us -> 38.2 us
  transfers between devices with their start and end apart: 18 -> 18, of which waited for: 2 -> 2; matrix products, arithmetic and copies ran while one was open for 37% -> 41% of each run, Pallas kernels for 0% -> 0%
where the time goes in v1:
time: 313 us; the launch traced here: 307 us
  starting transfers between devices  96.5 us (31%)
  local copies, waits for them, and re-layouts  78.8 us (25%)
  waiting for transfers between devices  71.8 us (23%)
  other arithmetic  41.9 us (13%)
  matrix products  14.9 us (5%)
    all_to_all x2, waiting for transfers between devices, far_field(): lax.all_to_all(jnp.stack([top_b[:, :, None]] * lax.axis_size(('row', 'col...  69.5 us
    all_to_all x2, starting transfers between devices, far_field(): lax.all_to_all(jnp.stack([top_b[:, :, None]] * lax.axis_size(('row', 'col...  47.5 us
    unnamed x239, local copies, waits for them, and re-layouts  38.2 us
    ppermute x6, starting transfers between devices, with_halo(): lax.ppermute(tail, axis, [(i, (i + 1) % count) for i in range(ends)])  22 us
    ppermute x6, starting transfers between devices, with_halo(): lax.ppermute(head, axis, [((i + 1) % count, i) for i in range(ends)])  18.7 us
    dot_general x25, matrix products, product(): return jnp.einsum(form, left, right, preferred_element_type=jnp.float32)  12.8 us
    slice x3, local copies, waits for them, and re-layouts, conj_flip(): return jnp.stack([flipped[0], -flipped[1]])  11.4 us
    ppermute x4, starting transfers between devices, from_behind(): return lax.ppermute(block, axis, route)  8.35 us
  transfers between devices with their start and end apart: 18, of which 2 were waited for; matrix products, arithmetic and copies ran while one was open for 41% of the time, Pallas kernels for 0%

profile of v1, /device:TPU:1, one launch (start us, length us, event | category | flops | bytes accessed | tf_op | source)
XLA Modules:
  0.0 307.0 jit_solution(17444984956518834403)
XLA Ops:
  5.0 1.3 collective-permute-start.5
  6.3 5.6 %collective-permute-start.4 = (f32[1,2,4,4,4,128]{5,4,3,2,1,0:T(4,128)}, f32[1,2,4,4,4,128]{5,4,3,2,1,0:T(4,128)}, u32[]{:S(2)}, u32[]{:S(2)}) collective-permute-start(f32[1,2,4,4,4,128]{5,4,3,2,1,0:T(4,128)} %pad_maximum_fusion.5), channel_id=1, source_target_pairs={{0,8},{8,16},{16,24},{24,32},{32,40},{40,48},{48,56},{56,64},{64,7... | collective-permute-start | bytes 196616 | tf_op jit(solution)/shard_map/ppermute | solution.py:17
  11.9 1.3 fusion.136
  13.2 1.3 collective-permute-start.1
  14.5 4.0 %collective-permute-start = (bf16[2,1,4,4,128]{4,3,2,1,0:T(4,128)(2,1)}, bf16[2,1,4,4,128]{4,3,2,1,0:T(4,128)(2,1)S(1)}, u32[]{:S(2)}, u32[]{:S(2)}) collective-permute-start(bf16[2,1,4,4,128]{4,3,2,1,0:T(4,128)(2,1)} %get-tuple-element.431), channel_id=1, source_target_pairs={{0,8},{8,16},{16,24},{24,32},{32,40},{40,48},{48,56},{56,64},{64,7... | collective-permute-start | bytes 24584 | tf_op jit(solution)/shard_map/ppermute | solution.py:17
  25.3 1.8 stack.775
  27.1 27.0 %all-to-all-start.1 = ((bf16[512,1,2,1,4,256]{5,4,3,2,1,0:T(4,128)(2,1)}), bf16[512,1,2,1,4,256]{5,4,3,2,1,0:T(4,128)(2,1)}, u32[]{:S(2)}, u32[]{:S(2)}) async-start(bf16[512,1,2,1,4,256]{5,4,3,2,1,0:T(4,128)(2,1)} %stack.775), calls=%async_computation.1 | async-start | bytes 4194304 | tf_op jit(solution)/shard_map/all_to_all | solution.py:139
  54.7 1.7 collective-permute-start.13
  57.8 6.3 %fusion.125 = (bf16[1,127,15,256]{3,0,2,1:T(2,128)(2,1)}, bf16[1,127,15,256]{3,0,2,1:T(2,128)(2,1)S(1)}) fusion(bf16[2,127,15,256]{3,0,2,1:T(2,128)(2,1)} %param.47), kind=kLoop, calls=%fused_computation.445 | loop fusion | bytes 3901440 | tf_op jit(solution)/shard_map/slice | solution.py:38
  64.1 3.3 %reverse_negate_fusion = bf16[1,127,15,256]{3,0,2,1:T(2,128)(2,1)} fusion(bf16[1,127,15,256]{3,0,2,1:T(2,128)(2,1)S(1)} %get-tuple-element.296), kind=kLoop, calls=%fused_computation.19 | loop fusion | flops 1463040 | bytes 1950720 | tf_op jit(solution)/shard_map/neg | solution.py:38
  67.4 4.9 %slice.1246 = bf16[1,127,15,256]{3,0,2,1:T(2,128)(2,1)} reverse(bf16[1,127,15,256]{3,0,2,1:T(2,128)(2,1)} %get-tuple-element.295), dimensions={1,2} | reverse | bytes 1950720 | tf_op jit(solution)/shard_map/slice | solution.py:38
  72.9 1.8 fusion.131
  77.8 1.4 and_reduce_fusion
  79.2 1.2 add_dynamic-update-slice_fusion
  80.4 1.9 fusion.63
  84.7 6.7 %maximum_bitcast_fusion = bf16[2,1905,256]{2,0,1:T(2,128)(2,1)} fusion(bf16[1,1,1905,256]{3,1,2,0:T(2,128)(2,1)} %bitcast.1065, bf16[1,1,1905,256]{3,1,2,0:T(2,128)(2,1)} %bitcast.1066), kind=kLoop, calls=%fused_computation.18 | loop fusion | flops 3901440 | bytes 3901440 | tf_op jit(solution)/shard_map/jit(_take)/Arg_0.13 | solution.py:150
  93.2 4.3 %gather_fusion.1 = bf16[512,2,256]{2,1,0:T(2,128)(2,1)} fusion(bf16[2,1905,256]{2,0,1:T(2,128)(2,1)} %maximum_bitcast_fusion, s32[1024]{0:T(1024)S(1)} %pad_clamp_fusion), kind=kCustom, calls=%fused_computation.1.clone | custom fusion | bytes 1050624 | tf_op jit(solution)/shard_map/jit(_take)/gather | solution.py:150
  97.4 3.6 %gather_fusion = bf16[512,2,256]{2,1,0:T(2,128)(2,1)S(1)} fusion(bf16[2,1905,256]{2,0,1:T(2,128)(2,1)} %bitcast.1063, s32[1024]{0:T(1024)} %copy-done.84), kind=kCustom, calls=%fused_computation.clone | custom fusion | bytes 1050624 | tf_op jit(solution)/shard_map/jit(_take)/gather | solution.py:150
  101.1 1.5 copy.425
  102.6 1.7 copy_bitcast_fusion.43
  104.3 1.6 copy_bitcast_fusion.41
  105.9 1.6 copy_bitcast_fusion.33
  117.9 1.8 fusion.45
  120.6 1.4 fusion.49
  122.1 6.3 %collective-permute-start.3 = (bf16[2,6,1,4,128]{4,3,2,1,0:T(4,128)(2,1)S(1)}, bf16[2,6,1,4,128]{4,3,2,1,0:T(4,128)(2,1)S(1)}, u32[]{:S(2)}, u32[]{:S(2)}) collective-permute-start(bf16[2,6,1,4,128]{4,3,2,1,0:T(4,128)(2,1)S(1)} %get-tuple-element.419), channel_id=1, source_target_pairs={{1,0},{2,1},{3,2},{4,3},{5,4},{6,5},{7,6},{9,8},{10,9},{11,10},{12... | collective-permute-start | bytes 36872 | tf_op jit(solution)/shard_map/ppermute | solution.py:19
  128.4 1.9 collective-permute-start.2
  151.0 4.9 %collective-permute-start.12 = (f32[1,2,4,4,4,128]{5,4,3,2,1,0:T(4,128)}, f32[1,2,4,4,4,128]{5,4,3,2,1,0:T(4,128)}, u32[]{:S(2)}, u32[]{:S(2)}) collective-permute-start(f32[1,2,4,4,4,128]{5,4,3,2,1,0:T(4,128)} %pad_maximum_fusion.6), channel_id=1, source_target_pairs={{0,8},{8,16},{16,24},{24,32},{32,40},{40,48},{48,56},{56,64},{64,7... | collective-permute-start | bytes 196616 | tf_op jit(solution)/shard_map/ppermute | solution.py:17
  155.9 1.9 collective-permute-start.8
  161.4 3.8 %stack.599 = bf16[9,2,4,4,4,128]{5,0,4,1,3,2:T(8,128)(2,1)} concatenate(bf16[1,2,4,4,4,128]{5,0,4,1,3,2:T(2,128)(2,1)S(1)} %copy.249, bf16[1,2,4,4,4,128]{5,0,4,1,3,2:T(2,128)(2,1)S(1)} %copy.250, bf16[1,2,4,4,4,128]{5,0,4,1,3,2:T(2,128)(2,1)} %copy.251, bf16[1,2,4,4,4,128]{5,0,4,1,3,2:T(2,128)(2,1)} %copy.252, bf16[1,2,4,4,4,128]{5,0,4,1,3,2:T(2,128)(2,1)S(1)} %copy.253, ...), dimensions={0} | concatenate | bytes 589824 | tf_op jit(solution)/shard_map/stack | solution.py:51
  165.1 1.3 fusion.10
  168.4 1.3 collective-permute-start.9
  170.8 2.3 collective-permute-done.9
  173.0 2.7 collective-permute-start.10
  175.8 1.8 stack.682
  177.6 20.5 %all-to-all-start = ((bf16[512,1,2,1,4,256]{5,4,3,2,1,0:T(4,128)(2,1)}), bf16[512,1,2,1,4,256]{5,4,3,2,1,0:T(4,128)(2,1)S(1)}, u32[]{:S(2)}, u32[]{:S(2)}) async-start(bf16[512,1,2,1,4,256]{5,4,3,2,1,0:T(4,128)(2,1)} %stack.682), calls=%async_computation | async-start | bytes 4194304 | tf_op jit(solution)/shard_map/all_to_all | solution.py:139
  199.5 6.2 %collective-permute-start.7 = (f32[1,2,12,4,4,128]{5,4,3,2,1,0:T(4,128)S(1)}, f32[1,2,12,4,4,128]{5,4,3,2,1,0:T(4,128)S(1)}, u32[]{:S(2)}, u32[]{:S(2)}) collective-permute-start(f32[1,2,12,4,4,128]{5,4,3,2,1,0:T(4,128)S(1)} %pad_maximum_fusion.2), channel_id=1, source_target_pairs={{1,0},{2,1},{3,2},{4,3},{5,4},{6,5},{7,6},{9,8},{10,9},{11,10},{12... | collective-permute-start | bytes 589832 | tf_op jit(solution)/shard_map/ppermute | solution.py:19
  205.7 1.9 collective-permute-start.6
  207.7 2.4 collective-permute-start.11
  211.0 1.9 collective-permute-start.15
  213.0 3.6 %collective-permute-start.14 = (f32[1,2,12,4,4,128]{5,4,3,2,1,0:T(4,128)S(1)}, f32[1,2,12,4,4,128]{5,4,3,2,1,0:T(4,128)S(1)}, u32[]{:S(2)}, u32[]{:S(2)}) collective-permute-start(f32[1,2,12,4,4,128]{5,4,3,2,1,0:T(4,128)S(1)} %pad_maximum_fusion.3), channel_id=1, source_target_pairs={{0,1},{1,2},{2,3},{3,4},{4,5},{5,6},{6,7},{8,9},{9,10},{10,11},{11... | collective-permute-start | bytes 589832 | tf_op jit(solution)/shard_map/ppermute | solution.py:17
  216.8 1.2 pad_maximum_fusion
  220.5 1.2 subtract_reduce_fusion.31
  221.9 1.2 pad_maximum_fusion.1
  223.2 1.8 subtract_reduce_fusion.6
  226.5 1.2 subtract_reduce_fusion.15
  227.9 3.1 %fusion.6 = (f32[256,4]{0,1:T(4,128)S(1)}, f32[256,4]{0,1:T(4,128)S(1)}, f32[256,4]{0,1:T(4,128)S(1)}, f32[256,4]{0,1:T(4,128)S(1)}) fusion(f32[256,512]{0,1:T(8,128)S(1)} %copy-done.4, bf16[1,2,512,4,256]{4,3,1,2,0:T(4,128)(2,1)} %bitcast.281, f32[256,512]{0,1:T(8,128)S(1)} %copy-done.3), kind=kLoop, calls=%fused_computation.16 | loop fusion | flops 5238784 | bytes 3162112 | tf_op jit(solution)/shard_map/snq,snmq->smq/dot_general | solution.py:157
  231.0 69.5 %all-to-all-done = bf16[512,1,2,1,4,256]{5,4,3,2,1,0:T(4,128)(2,1)S(1)} async-done(((bf16[512,1,2,1,4,256]{5,4,3,2,1,0:T(4,128)(2,1)}), bf16[512,1,2,1,4,256]{5,4,3,2,1,0:T(4,128)(2,1)S(1)}, u32[]{:S(2)}, u32[]{:S(2)}) %all-to-all-start) | async-done | bytes 2097184 | tf_op jit(solution)/shard_map/all_to_all | solution.py:139
  300.6 3.0 fusion.2
  (395 shorter events, 68.0 us)
Async XLA Ops:
  0.6 23.3 %copy-start = (f32[256,128]{1,0:T(8,128)S(1)}, f32[256,128]{1,0:T(8,128)}, u32[]{:S(2)}) copy-start(f32[256,128]{1,0:T(8,128)} %param.44) | copy-start | bytes 393220
  5.0 193.3 %collective-permute-start.5 = (f32[1,2,4,4,4,128]{5,4,3,2,1,0:T(4,128)}, f32[1,2,4,4,4,128]{5,4,3,2,1,0:T(4,128)}, u32[]{:S(2)}, u32[]{:S(2)}) collective-permute-start(f32[1,2,4,4,4,128]{5,4,3,2,1,0:T(4,128)} %pad_maximum_fusion.5), channel_id=1, source_target_pairs={{8,0},{16,8},{24,16},{32,24},{40,32},{48,40},{56,48},{64,56},{72,6... | collective-permute-start | bytes 196616 | tf_op jit(solution)/shard_map/ppermute | solution.py:19
  6.3 192.0 %collective-permute-start.4 = (f32[1,2,4,4,4,128]{5,4,3,2,1,0:T(4,128)}, f32[1,2,4,4,4,128]{5,4,3,2,1,0:T(4,128)}, u32[]{:S(2)}, u32[]{:S(2)}) collective-permute-start(f32[1,2,4,4,4,128]{5,4,3,2,1,0:T(4,128)} %pad_maximum_fusion.5), channel_id=1, source_target_pairs={{0,8},{8,16},{16,24},{24,32},{32,40},{40,48},{48,56},{56,64},{64,7... | collective-permute-start | bytes 196616 | tf_op jit(solution)/shard_map/ppermute | solution.py:17
  13.2 108.7 %collective-permute-start.1 = (bf16[2,1,4,4,128]{4,3,2,1,0:T(4,128)(2,1)}, bf16[2,1,4,4,128]{4,3,2,1,0:T(4,128)(2,1)S(1)}, u32[]{:S(2)}, u32[]{:S(2)}) collective-permute-start(bf16[2,1,4,4,128]{4,3,2,1,0:T(4,128)(2,1)} %get-tuple-element.430), channel_id=1, source_target_pairs={{8,0},{16,8},{24,16},{32,24},{40,32},{48,40},{56,48},{64,56},{72,6... | collective-permute-start | bytes 24584 | tf_op jit(solution)/shard_map/ppermute | solution.py:19
  14.5 107.4 %collective-permute-start = (bf16[2,1,4,4,128]{4,3,2,1,0:T(4,128)(2,1)}, bf16[2,1,4,4,128]{4,3,2,1,0:T(4,128)(2,1)S(1)}, u32[]{:S(2)}, u32[]{:S(2)}) collective-permute-start(bf16[2,1,4,4,128]{4,3,2,1,0:T(4,128)(2,1)} %get-tuple-element.431), channel_id=1, source_target_pairs={{0,8},{8,16},{16,24},{24,32},{32,40},{40,48},{48,56},{56,64},{64,7... | collective-permute-start | bytes 24584 | tf_op jit(solution)/shard_map/ppermute | solution.py:17
  27.1 29.4 %copy-start.1 = (bf16[2,4,4,2,128,128]{5,4,3,2,1,0:T(8,128)(2,1)S(1)}, bf16[2,4,4,2,128,128]{5,4,3,2,1,0:T(8,128)(2,1)}, u32[]{:S(2)}) copy-start(bf16[2,4,4,2,128,128]{5,4,3,2,1,0:T(8,128)(2,1)} %param.41) | copy-start | bytes 6291460
  27.1 29.4 %copy-start.9 = (bf16[2,4,4,4,128]{4,3,2,1,0:T(4,128)(2,1)S(1)}, bf16[2,4,4,4,128]{4,3,2,1,0:T(4,128)(2,1)}, u32[]{:S(2)}) copy-start(bf16[2,4,4,4,128]{4,3,2,1,0:T(4,128)(2,1)} %param.39) | copy-start | bytes 98308
  27.1 148.7 %all-to-all-start.1 = ((bf16[512,1,2,1,4,256]{5,4,3,2,1,0:T(4,128)(2,1)}), bf16[512,1,2,1,4,256]{5,4,3,2,1,0:T(4,128)(2,1)}, u32[]{:S(2)}, u32[]{:S(2)}) async-start(bf16[512,1,2,1,4,256]{5,4,3,2,1,0:T(4,128)(2,1)} %stack.775), calls=%async_computation.1 | async-start | bytes 4194304 | tf_op jit(solution)/shard_map/all_to_all | solution.py:139
  54.7 155.4 %collective-permute-start.13 = (f32[1,2,4,4,4,128]{5,4,3,2,1,0:T(4,128)}, f32[1,2,4,4,4,128]{5,4,3,2,1,0:T(4,128)}, u32[]{:S(2)}, u32[]{:S(2)}) collective-permute-start(f32[1,2,4,4,4,128]{5,4,3,2,1,0:T(4,128)} %pad_maximum_fusion.6), channel_id=1, source_target_pairs={{8,0},{16,8},{24,16},{32,24},{40,32},{48,40},{56,48},{64,56},{72,6... | collective-permute-start | bytes 196616 | tf_op jit(solution)/shard_map/ppermute | solution.py:19
  57.0 20.1 %copy-start.89 = (s32[2]{0:T(128)}, s32[2]{0:T(128)S(1)}, u32[]{:S(2)}) copy-start(s32[2]{0:T(128)S(1)} %iota_multiply_fusion) | copy-start | bytes 28
  72.3 20.9 %copy-start.84 = (s32[1024]{0:T(1024)}, s32[1024]{0:T(1024)S(1)}, u32[]{:S(2)}) copy-start(s32[1024]{0:T(1024)S(1)} %pad_clamp_fusion) | copy-start | bytes 12292
  102.6 8.3 %copy-start.73 = (f32[1,1,12,12,128]{4,1,3,2,0:T(1,128)S(1)}, f32[1,1,12,12,128]{4,1,3,2,0:T(1,128)}, u32[]{:S(2)}) copy-start(f32[1,1,12,12,128]{4,1,3,2,0:T(1,128)} %get-tuple-element.377) | copy-start | bytes 221188
  102.6 8.3 %copy-start.74 = (f32[1,1,12,12,128]{4,1,3,2,0:T(1,128)S(1)}, f32[1,1,12,12,128]{4,1,3,2,0:T(1,128)}, u32[]{:S(2)}) copy-start(f32[1,1,12,12,128]{4,1,3,2,0:T(1,128)} %get-tuple-element.378) | copy-start | bytes 221188
  120.5 9.8 %copy-start.86 = (bf16[4,256]{1,0:T(4,128)(2,1)S(1)}, bf16[4,256]{1,0:T(4,128)(2,1)}, u32[]{:S(2)}) copy-start(bf16[4,256]{1,0:T(4,128)(2,1)} %get-tuple-element.293) | copy-start | bytes 6148
  120.5 9.8 %copy-start.87 = (bf16[4,256]{1,0:T(4,128)(2,1)S(1)}, bf16[4,256]{1,0:T(4,128)(2,1)}, u32[]{:S(2)}) copy-start(bf16[4,256]{1,0:T(4,128)(2,1)} %get-tuple-element.294) | copy-start | bytes 6148
  122.1 29.0 %collective-permute-start.3 = (bf16[2,6,1,4,128]{4,3,2,1,0:T(4,128)(2,1)S(1)}, bf16[2,6,1,4,128]{4,3,2,1,0:T(4,128)(2,1)S(1)}, u32[]{:S(2)}, u32[]{:S(2)}) collective-permute-start(bf16[2,6,1,4,128]{4,3,2,1,0:T(4,128)(2,1)S(1)} %get-tuple-element.419), channel_id=1, source_target_pairs={{1,0},{2,1},{3,2},{4,3},{5,4},{6,5},{7,6},{9,8},{10,9},{11,10},{12... | collective-permute-start | bytes 36872 | tf_op jit(solution)/shard_map/ppermute | solution.py:19
  128.4 27.6 %collective-permute-start.2 = (bf16[2,6,1,4,128]{4,3,2,1,0:T(4,128)(2,1)S(1)}, bf16[2,6,1,4,128]{4,3,2,1,0:T(4,128)(2,1)S(1)}, u32[]{:S(2)}, u32[]{:S(2)}) collective-permute-start(bf16[2,6,1,4,128]{4,3,2,1,0:T(4,128)(2,1)S(1)} %get-tuple-element.420), channel_id=1, source_target_pairs={{0,1},{1,2},{2,3},{3,4},{4,5},{5,6},{6,7},{8,9},{9,10},{10,11},{11... | collective-permute-start | bytes 36872 | tf_op jit(solution)/shard_map/ppermute | solution.py:17
  151.0 59.1 %collective-permute-start.12 = (f32[1,2,4,4,4,128]{5,4,3,2,1,0:T(4,128)}, f32[1,2,4,4,4,128]{5,4,3,2,1,0:T(4,128)}, u32[]{:S(2)}, u32[]{:S(2)}) collective-permute-start(f32[1,2,4,4,4,128]{5,4,3,2,1,0:T(4,128)} %pad_maximum_fusion.6), channel_id=1, source_target_pairs={{0,8},{8,16},{16,24},{24,32},{32,40},{40,48},{48,56},{56,64},{64,7... | collective-permute-start | bytes 196616 | tf_op jit(solution)/shard_map/ppermute | solution.py:17
  155.9 11.7 %collective-permute-start.8 = (f32[2,6,4,128]{3,2,0,1:T(4,128)}, f32[2,6,4,128]{3,2,0,1:T(4,128)}, u32[]{:S(2)}, u32[]{:S(2)}) collective-permute-start(f32[2,6,4,128]{3,2,0,1:T(4,128)} %slice_bitcast_fusion.41), channel_id=1, source_target_pairs={{0,8},{8,16},{16,24},{24,32},{32,40},{40,48},{48,56},{56,64},{64,7... | collective-permute-start | bytes 73736 | tf_op jit(solution)/shard_map/ppermute | solution.py:29
  168.4 4.6 %collective-permute-start.9 = (f32[2,6,4,128]{3,2,0,1:T(4,128)S(1)}, f32[2,6,4,128]{3,2,0,1:T(4,128)S(1)}, u32[]{:S(2)}, u32[]{:S(2)}) collective-permute-start(f32[2,6,4,128]{3,2,0,1:T(4,128)S(1)} %slice_bitcast_fusion.40), channel_id=1, source_target_pairs={{8,0},{16,8},{24,16},{32,24},{40,32},{48,40},{56,48},{64,56},{72,6... | collective-permute-start | bytes 73736 | tf_op jit(solution)/shard_map/ppermute | solution.py:29
  173.0 34.6 %collective-permute-start.10 = (f32[2,4,4,128]{3,2,0,1:T(4,128)S(1)}, f32[2,4,4,128]{3,2,0,1:T(4,128)S(1)}, u32[]{:S(2)}, u32[]{:S(2)}) collective-permute-start(f32[2,4,4,128]{3,2,0,1:T(4,128)S(1)} %slice_bitcast_fusion.47), channel_id=1, source_target_pairs={{0,1},{1,2},{2,3},{3,4},{4,5},{5,6},{6,7},{8,9},{9,10},{10,11},{11... | collective-permute-start | bytes 49160 | tf_op jit(solution)/shard_map/ppermute | solution.py:29
  177.6 122.9 %all-to-all-start = ((bf16[512,1,2,1,4,256]{5,4,3,2,1,0:T(4,128)(2,1)}), bf16[512,1,2,1,4,256]{5,4,3,2,1,0:T(4,128)(2,1)S(1)}, u32[]{:S(2)}, u32[]{:S(2)}) async-start(bf16[512,1,2,1,4,256]{5,4,3,2,1,0:T(4,128)(2,1)} %stack.682), calls=%async_computation | async-start | bytes 4194304 | tf_op jit(solution)/shard_map/all_to_all | solution.py:139
  198.1 19.9 %copy-start.57 = (f32[12,12,128]{2,1,0:T(8,128)S(1)}, f32[12,12,128]{2,1,0:T(8,128)}, u32[]{:S(2)}) copy-start(f32[12,12,128]{2,1,0:T(8,128)} %get-tuple-element.454) | copy-start | bytes 221188
  198.1 19.9 %copy-start.58 = (f32[12,12,128]{2,1,0:T(8,128)S(1)}, f32[12,12,128]{2,1,0:T(8,128)}, u32[]{:S(2)}) copy-start(f32[12,12,128]{2,1,0:T(8,128)} %get-tuple-element.455) | copy-start | bytes 221188
  198.1 19.9 %copy-start.59 = (f32[12,12,128]{2,1,0:T(8,128)S(1)}, f32[12,12,128]{2,1,0:T(8,128)}, u32[]{:S(2)}) copy-start(f32[12,12,128]{2,1,0:T(8,128)} %get-tuple-element.452) | copy-start | bytes 221188
  198.2 19.9 %copy-start.60 = (f32[12,12,128]{2,1,0:T(8,128)S(1)}, f32[12,12,128]{2,1,0:T(8,128)}, u32[]{:S(2)}) copy-start(f32[12,12,128]{2,1,0:T(8,128)} %get-tuple-element.453) | copy-start | bytes 221188
  198.2 19.9 %copy-start.61 = (f32[12,12,128]{2,1,0:T(8,128)S(1)}, f32[12,12,128]{2,1,0:T(8,128)}, u32[]{:S(2)}) copy-start(f32[12,12,128]{2,1,0:T(8,128)} %get-tuple-element.450) | copy-start | bytes 221188
  198.2 19.9 %copy-start.62 = (f32[12,12,128]{2,1,0:T(8,128)S(1)}, f32[12,12,128]{2,1,0:T(8,128)}, u32[]{:S(2)}) copy-start(f32[12,12,128]{2,1,0:T(8,128)} %get-tuple-element.451) | copy-start | bytes 221188
  198.2 19.9 %copy-start.63 = (f32[12,12,128]{2,1,0:T(8,128)S(1)}, f32[12,12,128]{2,1,0:T(8,128)}, u32[]{:S(2)}) copy-start(f32[12,12,128]{2,1,0:T(8,128)} %get-tuple-element.442) | copy-start | bytes 221188
  198.2 19.9 %copy-start.64 = (f32[12,12,128]{2,1,0:T(8,128)S(1)}, f32[12,12,128]{2,1,0:T(8,128)}, u32[]{:S(2)}) copy-start(f32[12,12,128]{2,1,0:T(8,128)} %get-tuple-element.443) | copy-start | bytes 221188
  198.2 20.7 %copy-start.21 = (f32[12,12,128]{2,1,0:T(8,128)S(1)}, f32[12,12,128]{2,1,0:T(8,128)}, u32[]{:S(2)}) copy-start(f32[12,12,128]{2,1,0:T(8,128)} %get-tuple-element.460) | copy-start | bytes 221188
  198.2 20.7 %copy-start.22 = (f32[12,12,128]{2,1,0:T(8,128)S(1)}, f32[12,12,128]{2,1,0:T(8,128)}, u32[]{:S(2)}) copy-start(f32[12,12,128]{2,1,0:T(8,128)} %get-tuple-element.461) | copy-start | bytes 221188
  198.2 20.7 %copy-start.25 = (f32[12,12,128]{2,1,0:T(8,128)S(1)}, f32[12,12,128]{2,1,0:T(8,128)}, u32[]{:S(2)}) copy-start(f32[12,12,128]{2,1,0:T(8,128)} %get-tuple-element.458) | copy-start | bytes 221188
  198.2 20.7 %copy-start.26 = (f32[12,12,128]{2,1,0:T(8,128)S(1)}, f32[12,12,128]{2,1,0:T(8,128)}, u32[]{:S(2)}) copy-start(f32[12,12,128]{2,1,0:T(8,128)} %get-tuple-element.459) | copy-start | bytes 221188
  198.2 20.7 %copy-start.30 = (f32[12,12,128]{2,1,0:T(8,128)S(1)}, f32[12,12,128]{2,1,0:T(8,128)}, u32[]{:S(2)}) copy-start(f32[12,12,128]{2,1,0:T(8,128)} %get-tuple-element.456) | copy-start | bytes 221188
  198.3 20.7 %copy-start.31 = (f32[12,12,128]{2,1,0:T(8,128)S(1)}, f32[12,12,128]{2,1,0:T(8,128)}, u32[]{:S(2)}) copy-start(f32[12,12,128]{2,1,0:T(8,128)} %get-tuple-element.457) | copy-start | bytes 221188
  198.3 20.7 %copy-start.34 = (f32[12,12,128]{2,1,0:T(8,128)S(1)}, f32[12,12,128]{2,1,0:T(8,128)}, u32[]{:S(2)}) copy-start(f32[12,12,128]{2,1,0:T(8,128)} %get-tuple-element.444) | copy-start | bytes 221188
  198.3 20.7 %copy-start.35 = (f32[12,12,128]{2,1,0:T(8,128)S(1)}, f32[12,12,128]{2,1,0:T(8,128)}, u32[]{:S(2)}) copy-start(f32[12,12,128]{2,1,0:T(8,128)} %get-tuple-element.445) | copy-start | bytes 221188
  198.3 20.7 %copy-start.39 = (f32[12,12,128]{2,1,0:T(8,128)S(1)}, f32[12,12,128]{2,1,0:T(8,128)}, u32[]{:S(2)}) copy-start(f32[12,12,128]{2,1,0:T(8,128)} %get-tuple-element.446) | copy-start | bytes 221188
  198.3 20.7 %copy-start.40 = (f32[12,12,128]{2,1,0:T(8,128)S(1)}, f32[12,12,128]{2,1,0:T(8,128)}, u32[]{:S(2)}) copy-start(f32[12,12,128]{2,1,0:T(8,128)} %get-tuple-element.447) | copy-start | bytes 221188
  198.3 20.7 %copy-start.43 = (f32[12,12,128]{2,1,0:T(8,128)S(1)}, f32[12,12,128]{2,1,0:T(8,128)}, u32[]{:S(2)}) copy-start(f32[12,12,128]{2,1,0:T(8,128)} %get-tuple-element.448) | copy-start | bytes 221188
  198.3 20.7 %copy-start.44 = (f32[12,12,128]{2,1,0:T(8,128)S(1)}, f32[12,12,128]{2,1,0:T(8,128)}, u32[]{:S(2)}) copy-start(f32[12,12,128]{2,1,0:T(8,128)} %get-tuple-element.449) | copy-start | bytes 221188
  199.5 17.3 %collective-permute-start.7 = (f32[1,2,12,4,4,128]{5,4,3,2,1,0:T(4,128)S(1)}, f32[1,2,12,4,4,128]{5,4,3,2,1,0:T(4,128)S(1)}, u32[]{:S(2)}, u32[]{:S(2)}) collective-permute-start(f32[1,2,12,4,4,128]{5,4,3,2,1,0:T(4,128)S(1)} %pad_maximum_fusion.2), channel_id=1, source_target_pairs={{1,0},{2,1},{3,2},{4,3},{5,4},{6,5},{7,6},{9,8},{10,9},{11,10},{12... | collective-permute-start | bytes 589832 | tf_op jit(solution)/shard_map/ppermute | solution.py:19
  205.7 11.1 %collective-permute-start.6 = (f32[1,2,12,4,4,128]{5,4,3,2,1,0:T(4,128)S(1)}, f32[1,2,12,4,4,128]{5,4,3,2,1,0:T(4,128)S(1)}, u32[]{:S(2)}, u32[]{:S(2)}) collective-permute-start(f32[1,2,12,4,4,128]{5,4,3,2,1,0:T(4,128)S(1)} %pad_maximum_fusion.2), channel_id=1, source_target_pairs={{0,1},{1,2},{2,3},{3,4},{4,5},{5,6},{6,7},{8,9},{9,10},{10,11},{11... | collective-permute-start | bytes 589832 | tf_op jit(solution)/shard_map/ppermute | solution.py:17
  207.7 9.0 %collective-permute-start.11 = (f32[2,4,4,128]{3,2,0,1:T(4,128)S(1)}, f32[2,4,4,128]{3,2,0,1:T(4,128)S(1)}, u32[]{:S(2)}, u32[]{:S(2)}) collective-permute-start(f32[2,4,4,128]{3,2,0,1:T(4,128)S(1)} %slice_bitcast_fusion.46), channel_id=1, source_target_pairs={{1,0},{2,1},{3,2},{4,3},{5,4},{6,5},{7,6},{9,8},{10,9},{11,10},{12... | collective-permute-start | bytes 49160 | tf_op jit(solution)/shard_map/ppermute | solution.py:29
  211.0 10.8 %collective-permute-start.15 = (f32[1,2,12,4,4,128]{5,4,3,2,1,0:T(4,128)S(1)}, f32[1,2,12,4,4,128]{5,4,3,2,1,0:T(4,128)S(1)}, u32[]{:S(2)}, u32[]{:S(2)}) collective-permute-start(f32[1,2,12,4,4,128]{5,4,3,2,1,0:T(4,128)S(1)} %pad_maximum_fusion.3), channel_id=1, source_target_pairs={{1,0},{2,1},{3,2},{4,3},{5,4},{6,5},{7,6},{9,8},{10,9},{11,10},{12... | collective-permute-start | bytes 589832 | tf_op jit(solution)/shard_map/ppermute | solution.py:19
  213.0 8.9 %collective-permute-start.14 = (f32[1,2,12,4,4,128]{5,4,3,2,1,0:T(4,128)S(1)}, f32[1,2,12,4,4,128]{5,4,3,2,1,0:T(4,128)S(1)}, u32[]{:S(2)}, u32[]{:S(2)}) collective-permute-start(f32[1,2,12,4,4,128]{5,4,3,2,1,0:T(4,128)S(1)} %pad_maximum_fusion.3), channel_id=1, source_target_pairs={{0,1},{1,2},{2,3},{3,4},{4,5},{5,6},{6,7},{8,9},{9,10},{10,11},{11... | collective-permute-start | bytes 589832 | tf_op jit(solution)/shard_map/ppermute | solution.py:17
  231.0 72.9 %copy-start.8 = (bf16[2,128,128]{2,1,0:T(8,128)(2,1)S(1)}, bf16[2,128,128]{2,1,0:T(8,128)(2,1)}, u32[]{:S(2)}) copy-start(bf16[2,128,128]{2,1,0:T(8,128)(2,1)} %param.43) | copy-start | bytes 196612
  (62 other events, 261.5 us)
